TPU v7x, 512 devices: a whole 4x4x16 slice. The times are simulated.
512 devices in a mesh: ref: 16 (over y_hi, x, core), dom: 32 (over y_lo, z).
Axes of the slice: x: 4, y: 4 (y_hi: 2, y_lo: 2; y = y_hi * 2 + y_lo), z: 16, core: 2. Of those that a mesh axis runs over, the one named last changes fastest.
Arguments:
- particles: bfloat16 [16384, 4096], P(('ref', 'dom'))
- inv_noise: float32 [16384], P(('ref', 'dom')), may hold values from 1 to 6
- candidates: int32 [16384, 8], P(('ref', 'dom')), may hold values from 0 to 127, as said below
- offsets: int32 [9, 2], replicated, may hold values from -2 to 2, as said below
- references: bfloat16 [128, 4096], P('ref')
Outputs:
- refreshed: bfloat16 [128, 4096], P('ref', 'dom')
- log_evidence: float32 [16384], P(('ref', 'dom'))
Inputs may be any that keep to these rules, and one draw needn't show every extreme that they name: `candidates`: each row names 8 different classes; class loads are uneven. `offsets`: 9 different shifts.
All inputs are finite; a program needn't handle non-finite values.
Results may differ from a plain program's by a relative error of at most 0.0038.
Values may be sent and summed in bfloat16 or wider, within the bound.
No kernel may reach another device: no remote copies, remote signals or barrier semaphores. Data moves between devices by JAX's collectives and lax.ppermute only.
A program may use at most 64 MiB of HBM per device.

v0:
```python
import jax
import jax.numpy as jnp
from jax import lax
from jax.sharding import PartitionSpec as P

SIDE = 64


def flat_roll(images, row_move, col_move):
    pixels = SIDE * SIDE
    moved = jnp.roll(images, row_move * SIDE, axis=1)
    col_mod = jnp.mod(col_move, SIDE)
    column = jnp.arange(pixels, dtype=jnp.int32) % SIDE
    inside = jnp.roll(moved, col_mod, axis=1)
    wrapped = jnp.roll(moved, col_mod - SIDE, axis=1)
    return jnp.where((column >= col_mod)[None, :], inside, wrapped)


def roll_set(images, offsets, sign):
    translated_image = []
    for shift_idx in range(offsets.shape[0]):
        translated_image.append(
            flat_roll(images, sign * offsets[shift_idx, 0], sign * offsets[shift_idx, 1])
        )
    return jnp.stack(translated_image, axis=1)


def per_device(particles, inv_noise, candidates, offsets, references):
    tile_size = references.shape[0]
    all_classes = tile_size * lax.axis_size("ref")
    stacked = roll_set(particles, offsets, -1)
    tile_rows = lax.all_gather(references, "ref", axis=0, tiled=True)
    tile_float = tile_rows.astype(jnp.float32)
    norms = jnp.sum(tile_float * tile_float, axis=1)
    translated_image = roll_set(tile_rows, offsets, 1)
    match_score = jnp.einsum(
        "vi,jti->vtj", particles, translated_image, preferred_element_type=jnp.float32
    )
    update = match_score - 0.5 * norms[None, None, :]
    score = inv_noise[:, None, None] * update
    classes = jnp.arange(all_classes, dtype=jnp.int32)
    permitted_mask = jnp.any(candidates[:, :, None] == classes[None, None, :], axis=1)
    masked = jnp.where(permitted_mask[:, None, :], score, -1e30)
    peak_val = jnp.max(masked, axis=(1, 2))
    denom_sum = jnp.sum(jnp.exp(masked - peak_val[:, None, None]), axis=(1, 2))
    evidence = peak_val + jnp.log(denom_sum)
    weight = jnp.where(
        permitted_mask[:, None, :], jnp.exp(masked - evidence[:, None, None]), 0.0
    ).astype(jnp.bfloat16)
    summed = lax.psum_scatter(
        jnp.einsum("psk,psq->kq", weight, stacked, preferred_element_type=jnp.float32),
        "ref",
        scatter_dimension=0,
        tiled=True,
    )
    shares = lax.psum_scatter(summed, "dom", scatter_dimension=1, tiled=True)
    row_power = lax.psum(jnp.sum(shares * shares, axis=1), "dom")
    refreshed = (shares / jnp.sqrt(row_power[:, None] / (SIDE * SIDE) + 1e-06)).astype(jnp.bfloat16)
    return (refreshed, evidence)


def solution(mesh):
    in_specs = (
        P(("ref", "dom"), None),
        P(("ref", "dom")),
        P(("ref", "dom"), None),
        P(),
        P("ref", None),
    )
    out_specs = (P("ref", "dom"), P(("ref", "dom")))
    return jax.shard_map(
        per_device, mesh=mesh, in_specs=in_specs, out_specs=out_specs, check_vma=False
    )
```

profile of v0, /device:TPU:2, one launch (start us, length us, event | category | flops | bytes accessed | tf_op | source)
XLA Modules:
  0.0 408.3 jit_solution(2184901198757844488)
XLA Ops:
  7.2 0.0 all-gather.2.cloned.1.call-start
  7.2 0.7 all-gather.2.cloned.1.call-update
  7.9 0.0 reduce-scatter.3.cloned.1.call-start
  7.9 2.1 fusion.120
  39.1 1.0 constant_dynamic-update-slice_fusion.3
  40.1 1.0 constant_dynamic-update-slice_fusion.2
  41.5 1.0 constant_dynamic-slice_fusion.5
  42.5 0.6 fusion.91
  43.1 0.0 copy-start.2
  43.1 0.6 fusion.86
  43.7 0.6 fusion.81
  44.3 0.6 fusion.76
  44.9 0.6 fusion.71
  45.5 0.6 fusion.66
  46.1 0.6 fusion.61
  53.0 0.0 copy-done.2
  53.0 0.1 copy.8
  53.3 0.1 fusion.94
  53.4 0.6 fusion.56
  54.0 0.6 fusion.51
  54.6 21.1 %all-gather.2.cloned.1.call-done = bf16[128,4096]{1,0:T(8,128)(2,1)} async-done(((bf16[8,4096]{1,0:T(8,128)(2,1)}), bf16[128,4096]{1,0:T(8,128)(2,1)}) %all-gather.2.cloned.1.call-update) | async-done | bytes 1048592 | tf_op jit(solution)/shard_map/all_gather | solution.py:32
  75.7 0.0 copy-start
  75.7 1.6 multiply_reduce_fusion
  77.3 1.3 constant_dynamic-update-slice_fusion.1
  78.7 0.0 copy-done
  78.7 0.1 constant_dynamic-update-slice_fusion
  78.8 5.6 %constant_dynamic-slice_fusion.9 = (bf16[128,4096]{1,0:T(8,128)(2,1)S(1)}, bf16[128,4096]{1,0:T(8,128)(2,1)S(1)}, bf16[128,4096]{1,0:T(8,128)(2,1)S(1)}, bf16[12...) fusion(bf16[128,8192]{1,0:T(8,128)(2,1)S(1)} %constant_dynamic-, ...), kind=kLoop, calls=%fused_computation.190 | loop fusion | bytes 18874404 | tf_op jit(solution)/shard_map/jit(_roll_dynamic)/dynamic_slice | solution.py:11
  84.3 1.7 fusion.46
  86.0 1.8 fusion.41
  87.8 1.8 fusion.36
  89.6 1.8 fusion.31
  91.4 1.8 fusion.26
  93.2 2.0 fusion.21
  95.2 1.8 fusion.16
  96.9 0.0 copy-start.1
  97.0 0.0 copy-start.3
  97.0 1.8 fusion.11
  98.8 1.8 fusion.6
  100.6 0.0 copy-done.1
  100.6 0.0 copy-done.3
  100.6 3.0 fusion.121
  103.6 0.2 exponential_reduce_fusion
  103.8 0.0 copy-start.4
  103.8 2.2 convolution_bitcast_fusion
  106.0 0.0 copy-done.4
  106.0 0.0 reduce-scatter.3.cloned.1.call-update
  106.0 0.0 reduce-scatter.5.cloned.1.call-start
  106.1 93.1 %reduce-scatter.3.cloned.1.call-done = f32[8,4096]{1,0:T(8,128)} async-done(((f32[128,4096]{1,0:T(8,128)}), f32[8,4096]{1,0:T(8,128)}) %reduce-scatter.3.cloned.1.call-update) | async-done | bytes 131088 | tf_op jit(solution)/shard_map/reduce_scatter | solution.py:50
  199.2 0.0 reduce-scatter.5.cloned.1.call-update
  199.2 139.1 %reduce-scatter.5.cloned.1.call-done = f32[8,128]{1,0:T(8,128)} async-done(((f32[8,4096]{1,0:T(8,128)}), f32[8,128]{1,0:T(8,128)}) %reduce-scatter.5.cloned.1.call-update) | async-done | bytes 4112 | tf_op jit(solution)/shard_map/reduce_scatter | solution.py:56
  338.3 0.8 multiply_reduce_fusion.1
  339.1 61.3 %psum.7 = f32[8]{0:T(128)S(1)} all-reduce(f32[8]{0:T(128)S(1)} %multiply_reduce_fusion.1), channel_id=1, replica_groups=mesh['ref'=16,'dom'=32] {'dom'}, use_global_device_ids=true, to_apply=%region_7.10 | all-reduce | flops 8 | bytes 64 | tf_op jit(solution)/shard_map/psum | solution.py:57
  400.4 1.3 divide_convert_fusion
  (13 shorter events, 0.1 us)
Async XLA Ops:
  7.2 68.6 %all-gather.2.cloned.1.call-start = ((), (), s32[]{:S(2)}) async-start(), calls=%async_computation.2 | async-start | bytes 1114112 | tf_op jit(solution)/shard_map/all_gather | solution.py:32
  7.9 191.3 %reduce-scatter.3.cloned.1.call-start = ((), (), s32[]{:S(2)}) async-start(), calls=%async_computation.3 | async-start | bytes 2228224 | tf_op jit(solution)/shard_map/reduce_scatter | solution.py:50
  43.1 10.0 %copy-start.2 = (s32[32,8]{0,1:T(8,128)S(1)}, s32[32,8]{0,1:T(8,128)}, u32[]{:S(2)}) copy-start(s32[32,8]{0,1:T(8,128)} %param.11) | copy-start | bytes 3076
  75.7 2.9 copy-start
  96.9 3.6 copy-start.1
  97.0 3.6 copy-start.3
  103.8 2.2 copy-start.4
  106.0 232.3 %reduce-scatter.5.cloned.1.call-start = ((), (), s32[]{:S(2)}) async-start(), calls=%async_computation.4 | async-start | bytes 135168 | tf_op jit(solution)/shard_map/reduce_scatter | solution.py:56
Sparse Core Ops, SparseCore 0:
  11.3 64.4 all-gather.1
  106.1 92.9 reduce-scatter.2
  202.0 136.3 reduce-scatter.4
where the time goes:
time: 409 us; the launch traced here: 408 us
  waiting for transfers between devices  254 us (62%)
  blocking collectives  61.3 us (15%)
  between operations  49.9 us (12%)
  other arithmetic  25.7 us (6%)
  local copies, waits for them, and re-layouts  12 us (3%)
  matrix products  5.16 us (1%)
    reduce_scatter x1, waiting for transfers between devices, per_device(): shares = lax.psum_scatter(summed, 'dom', scatter_dimension=1, tiled=True)  139 us
    reduce_scatter x1, waiting for transfers between devices, per_device(): lax.psum_scatter(jnp.einsum('psk,psq->kq', weight, stacked, preferred_ele...  93.1 us
    psum x1, blocking collectives, per_device(): row_power = lax.psum(jnp.sum(shares * shares, axis=1), 'dom')  61.3 us
    all_gather x1, waiting for transfers between devices, per_device(): tile_rows = lax.all_gather(references, 'ref', axis=0, tiled=True)  21.1 us
    unnamed x16, other arithmetic  19.2 us
  transfers between devices with their start and end apart: 3, of which 3 were waited for; matrix products, arithmetic and copies ran while one was open for 3% of the time, Pallas kernels for 0%

commit v1 on v0

--- a/solution.py
+++ b/solution.py
@@ -54,7 +54,7 @@
         tiled=True,
     )
     shares = lax.psum_scatter(summed, "dom", scatter_dimension=1, tiled=True)
-    row_power = lax.psum(jnp.sum(shares * shares, axis=1), "dom")
+    row_power = jnp.sum(lax.all_gather(jnp.sum(shares * shares, axis=1), "dom"), axis=0)
     refreshed = (shares / jnp.sqrt(row_power[:, None] / (SIDE * SIDE) + 1e-06)).astype(jnp.bfloat16)
     return (refreshed, evidence)
 

time: 409 us -> 409 us (level)
  the two profiles are of different devices: /device:TPU:2 before, /device:TPU:6 now
where the time goes in v1:
time: 409 us
  waiting for transfers between devices  252 us (62%)
  blocking collectives  61.3 us (15%)
  between operations  50.3 us (12%)
  other arithmetic  25.8 us (6%)
  local copies, waits for them, and re-layouts  13.6 us (3%)
  matrix products  5.18 us (1%)
    reduce_scatter x1, waiting for transfers between devices, per_device(): shares = lax.psum_scatter(summed, 'dom', scatter_dimension=1, tiled=True)  137 us
    reduce_scatter x1, waiting for transfers between devices, per_device(): lax.psum_scatter(jnp.einsum('psk,psq->kq', weight, stacked, preferred_ele...  93.1 us
    unnamed x1, blocking collectives  61.3 us
    all_gather x1, waiting for transfers between devices, per_device(): tile_rows = lax.all_gather(references, 'ref', axis=0, tiled=True)  21.3 us
    unnamed x16, other arithmetic  19.2 us
  transfers between devices with their start and end apart: 3, of which 3 were waited for; matrix products, arithmetic and copies ran while one was open for 3% of the time, Pallas kernels for 0%

profile of v1, /device:TPU:6, one launch (start us, length us, event | category | flops | bytes accessed | tf_op | source)
XLA Modules:
  0.0 408.6 jit_solution(10187425489579379931)
XLA Ops:
  7.2 0.0 all-gather.3.cloned.1.call-start
  7.2 0.7 all-gather.3.cloned.1.call-update
  7.9 0.0 reduce-scatter.3.cloned.1.call-start
  7.9 2.1 fusion.120
  38.9 1.0 constant_dynamic-update-slice_fusion.3
  39.9 1.0 constant_dynamic-update-slice_fusion.2
  41.3 1.0 constant_dynamic-slice_fusion.5
  42.3 0.6 fusion.91
  42.9 0.0 copy-start.2
  42.9 0.6 fusion.86
  43.5 0.6 fusion.81
  44.1 0.6 fusion.76
  44.7 0.6 fusion.71
  45.3 0.6 fusion.66
  45.9 0.6 fusion.61
  52.8 0.0 copy-done.2
  52.8 0.1 copy.9
  53.1 0.1 fusion.94
  53.2 0.6 fusion.56
  53.8 0.6 fusion.51
  54.4 21.3 %all-gather.3.cloned.1.call-done = bf16[128,4096]{1,0:T(8,128)(2,1)} async-done(((bf16[8,4096]{1,0:T(8,128)(2,1)}), bf16[128,4096]{1,0:T(8,128)(2,1)}) %all-gather.3.cloned.1.call-update) | async-done | bytes 1048592 | tf_op jit(solution)/shard_map/all_gather | solution.py:32
  75.7 0.0 copy-start
  75.7 1.6 multiply_reduce_fusion
  77.3 1.3 constant_dynamic-update-slice_fusion.1
  78.6 0.0 copy-done
  78.6 0.1 constant_dynamic-update-slice_fusion
  78.7 5.6 %constant_dynamic-slice_fusion.9 = (bf16[128,4096]{1,0:T(8,128)(2,1)S(1)}, bf16[128,4096]{1,0:T(8,128)(2,1)S(1)}, bf16[128,4096]{1,0:T(8,128)(2,1)S(1)}, bf16[12...) fusion(bf16[128,8192]{1,0:T(8,128)(2,1)S(1)} %constant_dynamic-, ...), kind=kLoop, calls=%fused_computation.190 | loop fusion | bytes 18874404 | tf_op jit(solution)/shard_map/jit(_roll_dynamic)/dynamic_slice | solution.py:11
  84.3 1.7 fusion.46
  86.0 1.8 fusion.41
  87.7 1.8 fusion.36
  89.5 1.8 fusion.31
  91.3 1.8 fusion.26
  93.1 2.0 fusion.21
  95.1 1.8 fusion.16
  96.9 0.0 copy-start.1
  96.9 0.0 copy-start.3
  96.9 1.8 fusion.11
  98.7 1.8 fusion.6
  100.5 0.0 copy-done.1
  100.5 0.0 copy-done.3
  100.5 3.0 fusion.121
  103.5 0.2 exponential_reduce_fusion
  103.8 0.0 copy-start.4
  103.8 2.2 convolution_bitcast_fusion
  106.0 0.0 copy-done.4
  106.0 0.0 reduce-scatter.3.cloned.1.call-update
  106.0 0.0 reduce-scatter.5.cloned.1.call-start
  106.0 93.1 %reduce-scatter.3.cloned.1.call-done = f32[8,4096]{1,0:T(8,128)} async-done(((f32[128,4096]{1,0:T(8,128)}), f32[8,4096]{1,0:T(8,128)}) %reduce-scatter.3.cloned.1.call-update) | async-done | bytes 131088 | tf_op jit(solution)/shard_map/reduce_scatter | solution.py:50
  199.1 0.0 reduce-scatter.5.cloned.1.call-update
  199.2 1.3 dynamic-slice
  201.1 137.2 %reduce-scatter.5.cloned.1.call-done = f32[8,128]{1,0:T(8,128)} async-done(((f32[8,4096]{1,0:T(8,128)}), f32[8,128]{1,0:T(8,128)}) %reduce-scatter.5.cloned.1.call-update) | async-done | bytes 4112 | tf_op jit(solution)/shard_map/reduce_scatter | solution.py:56
  338.3 0.8 multiply_reduce_fusion.1
  339.1 0.2 dynamic-update-slice
  339.4 61.3 %all-reduce = f32[256]{0:T(256)S(1)} all-reduce(f32[256]{0:T(256)S(1)} %dynamic-update-slice), channel_id=2, replica_groups=mesh['ref'=16,'dom'=32] {'dom'}, use_global_device_ids=true, to_apply=%add | all-reduce | flops 256 | bytes 2048
  400.6 0.1 reshape.123
  400.8 1.3 divide_convert_fusion
  (15 shorter events, 0.2 us)
Async XLA Ops:
  7.2 68.5 %all-gather.3.cloned.1.call-start = ((), (), s32[]{:S(2)}) async-start(), calls=%async_computation.2 | async-start | bytes 1114112 | tf_op jit(solution)/shard_map/all_gather | solution.py:32
  7.9 191.2 %reduce-scatter.3.cloned.1.call-start = ((), (), s32[]{:S(2)}) async-start(), calls=%async_computation.3 | async-start | bytes 2228224 | tf_op jit(solution)/shard_map/reduce_scatter | solution.py:50
  42.9 10.0 %copy-start.2 = (s32[32,8]{0,1:T(8,128)S(1)}, s32[32,8]{0,1:T(8,128)}, u32[]{:S(2)}) copy-start(s32[32,8]{0,1:T(8,128)} %param.11) | copy-start | bytes 3076
  75.7 2.9 copy-start
  96.9 3.6 copy-start.1
  96.9 3.6 copy-start.3
  103.8 2.2 copy-start.4
  106.0 232.3 %reduce-scatter.5.cloned.1.call-start = ((), (), s32[]{:S(2)}) async-start(), calls=%async_computation.4 | async-start | bytes 135168 | tf_op jit(solution)/shard_map/reduce_scatter | solution.py:56
Sparse Core Ops, SparseCore 0:
  11.3 64.3 all-gather.2
  106.1 92.9 reduce-scatter.2
  201.9 136.3 reduce-scatter.4
